TPU v7x, 512 devices: a whole 4x8x8 slice. The times are simulated.
512 devices in a mesh: row: 16 (over y, core), col: 32 (over z, x).
Axes of the slice: x: 4, y: 8, z: 8, core: 2. Of those that a mesh axis runs over, the one named last changes fastest.
Arguments:
- tokens: bfloat16 [1024, 8192], P('col', 'row'), may hold values from -6 to 6
- gate_weight: bfloat16 [8192, 16384], P('row', 'col'), may hold values from -0.09375 to 0.09375
- up_weight: bfloat16 [8192, 16384], P('row', 'col'), may hold values from -0.09375 to 0.09375
- down_weight: bfloat16 [16384, 8192], P('col', 'row'), may hold values from -0.0625 to 0.0625
- gate_mask: int32 [64, 128], P('row', 'col'), may hold values from 0 to 1, as said below
- up_mask: int32 [64, 128], P('row', 'col'), may hold values from 0 to 1, as said below
- down_mask: int32 [128, 64], P('col', 'row'), may hold values from 0 to 1, as said below
Outputs:
- mixed: bfloat16 [1024, 8192], P('col', 'row')
Inputs may be any that keep to these rules, and one draw needn't show every extreme that they name: `gate_mask`: each entry is 0 or 1; the share of ones differs from one block column of hidden units to another. `up_mask`: each entry is 0 or 1; the share of ones differs from one block column of hidden units to another. `down_mask`: each entry is 0 or 1; the share of ones differs from one block row of hidden units to another.
All inputs are finite; a program needn't handle non-finite values.
Results may differ from a plain program's by a relative error of at most 0.0049.
Values may be sent and summed in bfloat16 or wider, within the bound.
No kernel may reach another device: no remote copies, remote signals or barrier semaphores. Data moves between devices by JAX's collectives and lax.ppermute only.
A program may use at most 64 MiB of HBM per device.

v0:
```python
import jax
import jax.numpy as jnp
from jax import lax
from jax.sharding import Mesh
from jax.sharding import PartitionSpec as P

BLK = 128
ROW = ("y", "c")
COL = ("z", "x")


def widen(block_mask):
    rows_blocks, cols_blocks = block_mask.shape
    spread = jnp.broadcast_to(block_mask[:, None, :, None], (rows_blocks, BLK, cols_blocks, BLK))
    return spread.reshape(rows_blocks * BLK, cols_blocks * BLK).astype(jnp.bfloat16)


def swiglu(summed, hidden_cols):
    return (jax.nn.silu(summed[:, :hidden_cols]) * summed[:, hidden_cols:]).astype(jnp.bfloat16)


def gather_rows(x, axes):
    for axis in reversed(axes):
        x = lax.all_gather(x, axis, axis=0, tiled=True)
    return x


def on_device(tokens, gate_weight, up_weight, down_weight, gate_mask, up_mask, down_mask):
    hidden_cols = gate_weight.shape[1]
    both_weights = jnp.concatenate(
        [gate_weight * widen(gate_mask), up_weight * widen(up_mask)], axis=1
    )
    down_eff = down_weight * widen(down_mask)
    all_tokens = gather_rows(tokens, COL)
    n_y, n_c = (lax.axis_size("y"), lax.axis_size("c"))
    rows, feats = all_tokens.shape
    share = rows // (n_y * n_c)
    by_core = all_tokens.reshape(n_y, n_c, share, feats).transpose(1, 0, 2, 3).reshape(rows, feats)
    partial = jnp.dot(by_core, both_weights, preferred_element_type=jnp.float32)
    partial = lax.psum_scatter(partial, "c", scatter_dimension=0, tiled=True)
    summed = lax.psum_scatter(partial, "y", scatter_dimension=0, tiled=True)
    hidden_share = swiglu(summed, hidden_cols)
    hidden = gather_rows(hidden_share, ROW)
    partial_out = jnp.dot(hidden, down_eff, preferred_element_type=jnp.float32)
    for axis in COL:
        partial_out = lax.psum_scatter(partial_out, axis, scatter_dimension=0, tiled=True)
    return partial_out.astype(jnp.bfloat16)


def solution(mesh):
    n_row, n_col = mesh.devices.shape
    n_c = 2
    n_x = 4
    sub = Mesh(mesh.devices.reshape(n_row // n_c, n_c, n_col // n_x, n_x), ROW + COL)
    placed = (
        P(COL, ROW),
        P(ROW, COL),
        P(ROW, COL),
        P(COL, ROW),
        P(ROW, COL),
        P(ROW, COL),
        P(COL, ROW),
    )
    return jax.shard_map(
        on_device, mesh=sub, in_specs=placed, out_specs=P(COL, ROW), check_vma=False
    )
```

profile of v0, /device:TPU:8, one launch (start us, length us, event | category | flops | bytes accessed | tf_op | source)
XLA Modules:
  0.0 265.3 jit_solution(16039085546751924385)
XLA Ops:
  6.5 13.8 %all_gather.12 = bf16[128,512]{1,0:T(8,128)(2,1)} all-gather(bf16[32,512]{1,0:T(8,128)(2,1)} %param.7), channel_id=1, replica_groups=mesh['y'=8,'c'=2,'z'=8,'x'=4] {'x'}, dimensions={0}, use_global_device_ids=true | all-gather | bytes 163840 | tf_op jit(solution)/shard_map/all_gather | solution.py:24
  20.4 0.0 reduce-scatter.7.cloned.1.call-start
  20.4 0.7 convert_element_type.29
  21.1 0.7 convert_element_type.27
  21.8 0.2 broadcast_in_dim.7
  22.0 0.2 broadcast_in_dim.6
  22.2 1.4 bitcast_multiply_fusion.2
  23.6 42.3 %all-gather.3.cloned.1.call-done = bf16[1024,512]{1,0:T(8,128)(2,1)} async-done(((bf16[128,512]{1,0:T(8,128)(2,1)}), bf16[1024,512]{1,0:T(8,128)(2,1)}) %all-gather.3.cloned.1.call-update) | async-done | bytes 1048592 | tf_op jit(solution)/shard_map/all_gather | solution.py:24
  65.8 1.3 copy.11
  67.2 3.3 %convolution_bitcast_fusion = f32[1024,1024]{0,1:T(8,128)} fusion(bf16[1024,512]{1,0:T(8,128)(2,1)S(1)} %bitcast.26, bf16[512,512]{1,0:T(8,128)(2,1)S(1)} %get-tuple-element.5, bf16[512,512]{1,0:T(8,128)(2,1)S(1)} %get-tuple-element.6), kind=kOutput, calls=%fused_computation | convolution fusion | flops 1075838976 | bytes 6291456 | tf_op jit(solution)/shard_map/dot_general | solution.py:39
  70.4 0.0 reduce-scatter.13.cloned.1.call-start
  70.5 18.3 %reduce-scatter.7.cloned.1.call-done = f32[512,1024]{0,1:T(8,128)} async-done(((f32[1024,1024]{0,1:T(8,128)}), f32[512,1024]{0,1:T(8,128)}) %reduce-scatter.7.cloned.1.call-update) | async-done | bytes 2097168 | tf_op jit(solution)/shard_map/reduce_scatter | solution.py:40
  88.8 2.9 %copy.14 = f32[512,1024]{1,0:T(8,128)} copy(f32[512,1024]{0,1:T(8,128)} %reduce-scatter.7.cloned.1.call-done) | data formatting | bytes 4194304
  91.7 0.0 all-gather.5.cloned.1.call-start
  91.8 46.0 %reduce-scatter.13.cloned.1.call-done = f32[64,1024]{1,0:T(8,128)} async-done(((f32[512,1024]{1,0:T(8,128)}), f32[64,1024]{1,0:T(8,128)}) %reduce-scatter.13.cloned.1.call-update) | async-done | bytes 262160 | tf_op jit(solution)/shard_map/reduce_scatter | solution.py:41
  137.8 1.0 fusion.5
  138.8 2.0 all_gather.14
  140.8 0.0 reduce-scatter.9.cloned.1.call-start
  140.9 40.2 %all-gather.5.cloned.1.call-done = bf16[1024,512]{1,0:T(8,128)(2,1)} async-done(((bf16[128,512]{1,0:T(8,128)(2,1)}), bf16[1024,512]{1,0:T(8,128)(2,1)}) %all-gather.5.cloned.1.call-update) | async-done | bytes 1048592 | tf_op jit(solution)/shard_map/all_gather | solution.py:24
  181.1 0.2 broadcast_in_dim.8
  181.4 3.3 %fusion.3 = f32[1024,512]{1,0:T(8,128)} fusion(bf16[1024,512]{1,0:T(8,128)(2,1)} %all-gather.5.cloned.1.call-done, bf16[512,512]{1,0:T(8,128)(2,1)S(1)} %copy-done, bf16[64,8,4,128]{3,2,1,0:T(4,128)(2,1)S(1)} %bitcast.24), kind=kOutput, calls=%fused_computation.5 | convolution fusion | flops 537133056 | bytes 4194304 | tf_op jit(solution)/shard_map/dot_general | solution.py:44
  184.7 45.6 %reduce-scatter.9.cloned.1.call-done = f32[128,512]{1,0:T(8,128)} async-done(((f32[1024,512]{1,0:T(8,128)}), f32[128,512]{1,0:T(8,128)}) %reduce-scatter.9.cloned.1.call-update) | async-done | bytes 262160 | tf_op jit(solution)/shard_map/reduce_scatter | solution.py:46
  230.3 26.7 %reduce-scatter.11.cloned.1.call-done = f32[32,512]{1,0:T(8,128)} async-done(((f32[128,512]{1,0:T(8,128)}), f32[32,512]{1,0:T(8,128)}) %reduce-scatter.11.cloned.1.call-update) | async-done | bytes 65552 | tf_op jit(solution)/shard_map/reduce_scatter | solution.py:46
  257.0 1.5 convert_element_type.34
  (13 shorter events, 0.2 us)
Async XLA Ops:
  6.5 59.3 %all-gather.3.cloned.1.call-start = ((), (), s32[]{:S(2)}) async-start(), calls=%async_computation.4 | async-start | bytes 1179648 | tf_op jit(solution)/shard_map/all_gather | solution.py:24
  20.4 68.4 %reduce-scatter.7.cloned.1.call-start = ((), (), s32[]{:S(2)}) async-start(), calls=%async_computation.5 | async-start | bytes 6291456 | tf_op jit(solution)/shard_map/reduce_scatter | solution.py:40
  70.4 67.3 %reduce-scatter.13.cloned.1.call-start = ((), (), s32[]{:S(2)}) async-start(), calls=%async_computation.9 | async-start | bytes 2359296 | tf_op jit(solution)/shard_map/reduce_scatter | solution.py:41
  91.7 49.2 %copy-start.1 = (s32[4,4]{1,0:T(4,128)S(1)}, s32[4,4]{1,0:T(4,128)}, u32[]{:S(2)}) copy-start(s32[4,4]{1,0:T(4,128)} %param.13) | copy-start | bytes 196
  91.7 89.6 %copy-start = (bf16[512,512]{1,0:T(8,128)(2,1)S(1)}, bf16[512,512]{1,0:T(8,128)(2,1)}, u32[]{:S(2)}) copy-start(bf16[512,512]{1,0:T(8,128)(2,1)} %param.10) | copy-start | bytes 1572868
  91.7 89.4 %all-gather.5.cloned.1.call-start = ((), (), s32[]{:S(2)}) async-start(), calls=%async_computation.6 | async-start | bytes 1179648 | tf_op jit(solution)/shard_map/all_gather | solution.py:24
  140.8 89.4 %reduce-scatter.9.cloned.1.call-start = ((), (), s32[]{:S(2)}) async-start(), calls=%async_computation.7 | async-start | bytes 2359296 | tf_op jit(solution)/shard_map/reduce_scatter | solution.py:46
  184.7 72.3 %reduce-scatter.11.cloned.1.call-start = ((), (), s32[]{:S(2)}) async-start(), calls=%async_computation.8 | async-start | bytes 327680 | tf_op jit(solution)/shard_map/reduce_scatter | solution.py:46
Sparse Core Ops, SparseCore 0:
  20.5 45.2 all-gather.2
  70.6 18.1 reduce-scatter.6
  91.8 45.8 reduce-scatter.12
  141.0 40.1 all-gather.4
  184.8 45.4 reduce-scatter.8
  232.9 23.9 reduce-scatter.10
where the time goes:
time: 266 us; the launch traced here: 265 us
  waiting for transfers between devices  219 us (82%)
  blocking collectives  15.8 us (6%)
  between operations  13.5 us (5%)
  matrix products  6.54 us (2%)
  other arithmetic  5.21 us (2%)
  local copies, waits for them, and re-layouts  4.87 us (2%)
    all_gather x2, waiting for transfers between devices, gather_rows(): x = lax.all_gather(x, axis, axis=0, tiled=True)  82.5 us
    reduce_scatter x2, waiting for transfers between devices, on_device(): lax.psum_scatter(partial_out, axis, scatter_dimension=0, tiled=True)  72.2 us
    reduce_scatter x1, waiting for transfers between devices, on_device(): summed = lax.psum_scatter(partial, 'y', scatter_dimension=0, tiled=True)  46 us
    reduce_scatter x1, waiting for transfers between devices, on_device(): partial = lax.psum_scatter(partial, 'c', scatter_dimension=0, tiled=True)  18.3 us
    all_gather x2, blocking collectives, gather_rows(): x = lax.all_gather(x, axis, axis=0, tiled=True)  15.8 us
  transfers between devices with their start and end apart: 6, of which 6 were waited for; matrix products, arithmetic and copies ran while one was open for 1% of the time, Pallas kernels for 0%

commit v1 on v0

--- a/solution.py
+++ b/solution.py
@@ -21,7 +21,9 @@
 
 def gather_rows(x, axes):
     for axis in reversed(axes):
-        x = lax.all_gather(x, axis, axis=0, tiled=True)
+        x = jnp.concatenate(
+            lax.all_to_all(jnp.stack([x] * lax.axis_size(axis)), axis, 0, 0), axis=0
+        )
     return x
 
 

time: 266 us -> 244 us (0.917)
  waiting for transfers between devices: 219 us -> 185 us
  starting transfers between devices: 0.21 us -> 15.9 us
  other arithmetic: 5.21 us -> 1.76 us
  local copies, waits for them, and re-layouts: 4.87 us -> 7.92 us
    all_gather x2 -> x0, waiting for transfers between devices: 82.5 us -> none  [gather_rows(): x = lax.all_gather(x, axis, axis=0, tiled=True)]
    all_to_all x0 -> x2, waiting for transfers between devices: none -> 54.2 us  [gather_rows(): lax.all_to_all(jnp.stack([x] * lax.axis_size(axis)), axis, 0, 0)]
    unnamed x6 -> x5, waiting for transfers between devices: 0.1 us -> 46.3 us
    reduce_scatter x1 -> x0, waiting for transfers between devices: 46 us -> none  [on_device(): summed = lax.psum_scatter(partial, 'y', scatter_dimension=0, tiled=True)]
    all_gather x2 -> x0, blocking collectives: 15.8 us -> none  [gather_rows(): x = lax.all_gather(x, axis, axis=0, tiled=True)]
    all_to_all x0 -> x2, starting transfers between devices: none -> 15.7 us  [gather_rows(): lax.all_to_all(jnp.stack([x] * lax.axis_size(axis)), axis, 0, 0)]
    all_to_all x0 -> x2, blocking collectives: none -> 14 us  [gather_rows(): lax.all_to_all(jnp.stack([x] * lax.axis_size(axis)), axis, 0, 0)]
    reduce_scatter x1, waiting for transfers between devices: 18.3 us -> 14.4 us  [on_device(): partial = lax.psum_scatter(partial, 'c', scatter_dimension=0, tiled=True)]
  transfers between devices with their start and end apart: 6 -> 6, of which waited for: 6 -> 6; matrix products, arithmetic and copies ran while one was open for 1% -> 0% of each run, Pallas kernels for 0% -> 0%
where the time goes in v1:
time: 244 us; the launch traced here: 243 us
  waiting for transfers between devices  185 us (76%)
  starting transfers between devices  15.9 us (7%)
  blocking collectives  14 us (6%)
  between operations  13.3 us (5%)
  local copies, waits for them, and re-layouts  7.92 us (3%)
  matrix products  5.31 us (2%)
    reduce_scatter x2, waiting for transfers between devices, on_device(): lax.psum_scatter(partial_out, axis, scatter_dimension=0, tiled=True)  70.4 us
    all_to_all x2, waiting for transfers between devices, gather_rows(): lax.all_to_all(jnp.stack([x] * lax.axis_size(axis)), axis, 0, 0)  54.2 us
    unnamed x5, waiting for transfers between devices  46.3 us
    all_to_all x2, starting transfers between devices, gather_rows(): lax.all_to_all(jnp.stack([x] * lax.axis_size(axis)), axis, 0, 0)  15.7 us
    reduce_scatter x1, waiting for transfers between devices, on_device(): partial = lax.psum_scatter(partial, 'c', scatter_dimension=0, tiled=True)  14.4 us
    all_to_all x2, blocking collectives, gather_rows(): lax.all_to_all(jnp.stack([x] * lax.axis_size(axis)), axis, 0, 0)  14 us
  transfers between devices with their start and end apart: 6, of which 6 were waited for; matrix products, arithmetic and copies ran while one was open for 0% of the time, Pallas kernels for 0%

profile of v1, /device:TPU:8, one launch (start us, length us, event | category | flops | bytes accessed | tf_op | source)
XLA Modules:
  0.0 243.4 jit_solution(12784983155712700515)
XLA Ops:
  6.5 0.8 stack.20
  7.3 10.1 %all_to_all.20 = bf16[4,32,512]{2,1,0:T(8,128)(2,1)S(1)} all-to-all(bf16[4,32,512]{2,1,0:T(8,128)(2,1)S(1)} %stack.20), channel_id=1, replica_groups=mesh['y'=8,'c'=2,'z'=8,'x'=4] {'x'}, dimensions={0} | all-to-all | bytes 262144 | tf_op jit(solution)/shard_map/all_to_all | solution.py:25
  17.4 1.1 stack.21
  18.5 10.3 %all-to-all-start.1 = ((bf16[8,128,512]{2,1,0:T(8,128)(2,1)}), bf16[8,128,512]{2,1,0:T(8,128)(2,1)S(1)}, u32[]{:S(2)}, u32[]{:S(2)}) async-start(bf16[8,128,512]{2,1,0:T(8,128)(2,1)} %stack.21), calls=%async_computation.1 | async-start | bytes 2097152 | tf_op jit(solution)/shard_map/all_to_all | solution.py:25
  28.9 0.2 broadcast_in_dim.6
  29.1 0.2 broadcast_in_dim.7
  29.3 0.2 bitcast_multiply_fusion.2
  29.5 26.6 %all-to-all-done.1 = bf16[8,128,512]{2,1,0:T(8,128)(2,1)S(1)} async-done(((bf16[8,128,512]{2,1,0:T(8,128)(2,1)}), bf16[8,128,512]{2,1,0:T(8,128)(2,1)S(1)}, u32[]{:S(2)}, u32[]{:S(2)}) %all-to-all-start.1) | async-done | bytes 1048608 | tf_op jit(solution)/shard_map/all_to_all | solution.py:25
  56.2 3.3 %convolution_bitcast_fusion = f32[1024,1024]{0,1:T(8,128)} fusion(bf16[1024,512]{1,0:T(8,128)(2,1)S(1)} %bitcast.32, bf16[512,512]{1,0:T(8,128)(2,1)S(1)} %get-tuple-element.7, bf16[512,512]{1,0:T(8,128)(2,1)S(1)} %get-tuple-element.8), kind=kOutput, calls=%fused_computation | convolution fusion | flops 1075838976 | bytes 6291456 | tf_op jit(solution)/shard_map/dot_general | solution.py:41
  59.5 14.4 %reduce-scatter.7.cloned.1.call-done = f32[512,1024]{0,1:T(8,128)} async-done(((f32[1024,1024]{0,1:T(8,128)}), f32[512,1024]{0,1:T(8,128)}) %reduce-scatter.7.cloned.1.call-update) | async-done | bytes 2097168 | tf_op jit(solution)/shard_map/reduce_scatter | solution.py:42
  74.0 2.9 %copy.13 = f32[512,1024]{1,0:T(8,128)} copy(f32[512,1024]{0,1:T(8,128)} %reduce-scatter.7.cloned.1.call-done) | data formatting | bytes 4194304
  76.9 46.2 %reduce-scatter.13.cloned.1.call-done = f32[64,1024]{1,0:T(8,128)} async-done(((f32[512,1024]{1,0:T(8,128)}), f32[64,1024]{1,0:T(8,128)}) %reduce-scatter.13.cloned.1.call-update) | async-done | bytes 262160
  123.1 1.0 fusion.7
  124.2 0.1 copy.16
  124.5 0.1 copy.12
  124.7 4.0 %all_to_all.21 = bf16[2,64,512]{2,1,0:T(8,128)(2,1)S(1)} all-to-all(bf16[2,64,512]{2,1,0:T(8,128)(2,1)S(1)} %copy.12), channel_id=1, replica_groups=mesh['y'=8,'c'=2,'z'=8,'x'=4] {'c'}, dimensions={0} | all-to-all | bytes 262144 | tf_op jit(solution)/shard_map/all_to_all | solution.py:25
  128.6 1.1 stack.24
  129.7 5.4 %all-to-all-start.3 = ((bf16[8,128,512]{2,1,0:T(8,128)(2,1)}), bf16[8,128,512]{2,1,0:T(8,128)(2,1)S(1)}, u32[]{:S(2)}, u32[]{:S(2)}) async-start(bf16[8,128,512]{2,1,0:T(8,128)(2,1)} %stack.24), calls=%async_computation.4 | async-start | bytes 2097152 | tf_op jit(solution)/shard_map/all_to_all | solution.py:25
  135.1 27.6 %all-to-all-done.3 = bf16[8,128,512]{2,1,0:T(8,128)(2,1)S(1)} async-done(((bf16[8,128,512]{2,1,0:T(8,128)(2,1)}), bf16[8,128,512]{2,1,0:T(8,128)(2,1)S(1)}, u32[]{:S(2)}, u32[]{:S(2)}) %all-to-all-start.3) | async-done | bytes 1048608 | tf_op jit(solution)/shard_map/all_to_all | solution.py:25
  162.7 0.2 broadcast_in_dim.8
  162.9 2.1 fusion.3
  165.1 43.2 %reduce-scatter.9.cloned.1.call-done = f32[128,512]{1,0:T(8,128)} async-done(((f32[1024,512]{1,0:T(8,128)}), f32[128,512]{1,0:T(8,128)}) %reduce-scatter.9.cloned.1.call-update) | async-done | bytes 262160 | tf_op jit(solution)/shard_map/reduce_scatter | solution.py:48
  208.3 27.1 %reduce-scatter.11.cloned.1.call-done = f32[32,512]{1,0:T(8,128)} async-done(((f32[128,512]{1,0:T(8,128)}), f32[32,512]{1,0:T(8,128)}) %reduce-scatter.11.cloned.1.call-update) | async-done | bytes 65552 | tf_op jit(solution)/shard_map/reduce_scatter | solution.py:48
  235.4 1.5 convert_element_type.34
  (27 shorter events, 0.6 us)
Async XLA Ops:
  6.5 22.3 %copy-start.3 = (s32[4,4]{1,0:T(4,128)S(1)}, s32[4,4]{1,0:T(4,128)}, u32[]{:S(2)}) copy-start(s32[4,4]{1,0:T(4,128)} %param.11) | copy-start | bytes 196
  6.5 22.3 %copy-start.4 = (s32[4,4]{1,0:T(4,128)S(1)}, s32[4,4]{1,0:T(4,128)}, u32[]{:S(2)}) copy-start(s32[4,4]{1,0:T(4,128)} %param.12) | copy-start | bytes 196
  17.4 11.9 %copy-start = (bf16[512,512]{1,0:T(8,128)(2,1)S(1)}, bf16[512,512]{1,0:T(8,128)(2,1)}, u32[]{:S(2)}) copy-start(bf16[512,512]{1,0:T(8,128)(2,1)} %param.9) | copy-start | bytes 1572868
  17.4 11.9 %copy-start.1 = (bf16[512,512]{1,0:T(8,128)(2,1)S(1)}, bf16[512,512]{1,0:T(8,128)(2,1)}, u32[]{:S(2)}) copy-start(bf16[512,512]{1,0:T(8,128)(2,1)} %param.8) | copy-start | bytes 1572868
  18.5 37.6 %all-to-all-start.1 = ((bf16[8,128,512]{2,1,0:T(8,128)(2,1)}), bf16[8,128,512]{2,1,0:T(8,128)(2,1)S(1)}, u32[]{:S(2)}, u32[]{:S(2)}) async-start(bf16[8,128,512]{2,1,0:T(8,128)(2,1)} %stack.21), calls=%async_computation.1 | async-start | bytes 2097152 | tf_op jit(solution)/shard_map/all_to_all | solution.py:25
  28.8 45.2 %reduce-scatter.7.cloned.1.call-start = ((), (), s32[]{:S(2)}) async-start(), calls=%async_computation.8 | async-start | bytes 6291456 | tf_op jit(solution)/shard_map/reduce_scatter | solution.py:42
  59.5 63.6 %reduce-scatter.13.cloned.1.call-start = ((), (), s32[]{:S(2)}) async-start(), calls=%async_computation.11 | async-start | bytes 2359296
  124.5 10.7 %copy-start.5 = (s32[4,4]{1,0:T(4,128)S(1)}, s32[4,4]{1,0:T(4,128)}, u32[]{:S(2)}) copy-start(s32[4,4]{1,0:T(4,128)} %param.13) | copy-start | bytes 196
  124.7 38.3 %copy-start.2 = (bf16[512,512]{1,0:T(8,128)(2,1)S(1)}, bf16[512,512]{1,0:T(8,128)(2,1)}, u32[]{:S(2)}) copy-start(bf16[512,512]{1,0:T(8,128)(2,1)} %param.10) | copy-start | bytes 1572868
  129.7 33.0 %all-to-all-start.3 = ((bf16[8,128,512]{2,1,0:T(8,128)(2,1)}), bf16[8,128,512]{2,1,0:T(8,128)(2,1)S(1)}, u32[]{:S(2)}, u32[]{:S(2)}) async-start(bf16[8,128,512]{2,1,0:T(8,128)(2,1)} %stack.24), calls=%async_computation.4 | async-start | bytes 2097152 | tf_op jit(solution)/shard_map/all_to_all | solution.py:25
  135.1 73.2 %reduce-scatter.9.cloned.1.call-start = ((), (), s32[]{:S(2)}) async-start(), calls=%async_computation.9 | async-start | bytes 2359296 | tf_op jit(solution)/shard_map/reduce_scatter | solution.py:48
  165.0 70.4 %reduce-scatter.11.cloned.1.call-start = ((), (), s32[]{:S(2)}) async-start(), calls=%async_computation.10 | async-start | bytes 327680 | tf_op jit(solution)/shard_map/reduce_scatter | solution.py:48
Sparse Core Ops, SparseCore 0:
  59.6 14.3 reduce-scatter.6
  77.0 46.0 reduce-scatter.12
  165.1 43.1 reduce-scatter.8
  211.0 24.4 reduce-scatter.10
